TPU v7x, 512 devices: a whole 4x8x8 slice. The times are simulated.
512 devices in a mesh: req: 128 (over y, z, core), tp: 4 (over x).
Axes of the slice: x: 4, y: 8, z: 8, core: 2. Of those that a mesh axis runs over, the one named last changes fastest.
Arguments:
- qkv_rows: bfloat16 [32768, 3, 1536], P('req', None, 'tp'), may hold values from -13 to 13
- row_request: int32 [32768], P('req'), may hold values from 0 to 127, as said below
- request_owner: int32 [128], replicated, may hold values from 0 to 127, each once
- cached_len: int32 [128], P('req'), may hold values from 0 to 1024
- page_table: int32 [128, 8], P('req'), may hold values from 0 to 7, as said below
- kv_pages: bfloat16 [1024, 2, 128, 1536], P('req', None, None, 'tp'), may hold values from -6 to 6
- residual: bfloat16 [32768, 3072], P('req', 'tp'), may hold values from -128 to 128
- out_weight: bfloat16 [1536, 3072], P('tp'), may hold values from -0.15625 to 0.15625
- norm_gain: bfloat16 [3072], P('tp'), may hold values from 0.5 to 1.5
Outputs:
- new_residual: bfloat16 [32768, 3072], P('req', 'tp')
- normed: bfloat16 [32768, 3072], P('req', 'tp')
Inputs may be any that keep to these rules, and one draw needn't show every extreme that they name: `row_request`: on every device at most 5 new tokens name the same request, and one request is named by exactly 5 tokens on every device. Half of the requests are named by exactly one token in all, and no two of those tokens lie on one device. `request_owner`: each device holds the cache of exactly one request. `page_table`: each row names every page of its device's pool once.
All inputs are finite; a program needn't handle non-finite values.
Results may differ from a plain program's by a relative error of at most 0.0093.
The roundings to bfloat16 on the way count: a program that leaves them out, or rounds other values in their place, can miss the bound.
Values may be sent and summed in bfloat16 or wider, within the bound.
No kernel may reach another device: no remote copies, remote signals or barrier semaphores. Data moves between devices by JAX's collectives and lax.ppermute only.
A program may use at most 64 MiB of HBM per device.

v0:
```python
import math
import jax
import jax.numpy as jnp
from jax import lax
from jax.sharding import PartitionSpec as P

D = 3072
HEAD_SIZE = 96
ROPE_BASE = 10000.0
EPS = 1e-05


def rope_tables(position):
    halves = HEAD_SIZE // 2
    inverse = ROPE_BASE ** (-2.0 * jnp.arange(halves, dtype=jnp.float32) / HEAD_SIZE)
    angles = position.astype(jnp.float32)[:, None] * inverse[None, :]
    cosine = jnp.concatenate([jnp.cos(angles), jnp.cos(angles)], axis=1)
    sine_tab = jnp.concatenate([jnp.sin(angles), jnp.sin(angles)], axis=1)
    return (cosine, sine_tab)


def rotate(field, cosine, sine_tab):
    halves = HEAD_SIZE // 2
    turned = jnp.concatenate([-field[..., halves:], field[..., :halves]], axis=-1)
    return field * cosine[:, None, :] + turned * sine_tab[:, None, :]


def attend_heads(grouped, cache_keys, cache_values, cosine, sine_tab, visible):
    score_scale = 1.0 / math.sqrt(HEAD_SIZE)
    query_rows_block = rotate(grouped[:, 0].astype(jnp.float32), cosine, sine_tab).astype(
        jnp.bfloat16
    )
    fresh_keys = rotate(grouped[:, 1].astype(jnp.float32), cosine, sine_tab).astype(jnp.bfloat16)
    gathered_keys = jnp.concatenate([cache_keys, fresh_keys], axis=0)
    gathered_values = jnp.concatenate([cache_values, grouped[:, 2]], axis=0)

    def one_head(head_parts):
        head_query, head_keys, head_values = head_parts
        logit_scores = (
            jnp.einsum("md,kd->mk", head_query, head_keys, preferred_element_type=jnp.float32)
            * score_scale
        )
        logit_scores = jnp.where(visible, logit_scores, -1e30)
        top_score = jnp.max(logit_scores, axis=1, keepdims=True)
        weight = jnp.exp(logit_scores - top_score)
        softmax_weights = (weight / jnp.sum(weight, axis=1, keepdims=True)).astype(jnp.bfloat16)
        return jnp.einsum(
            "mk,kd->md", softmax_weights, head_values, preferred_element_type=jnp.float32
        ).astype(jnp.bfloat16)

    heads_out = lax.map(
        one_head,
        (
            query_rows_block.transpose(1, 0, 2),
            gathered_keys.transpose(1, 0, 2),
            gathered_values.transpose(1, 0, 2),
        ),
    )
    return heads_out.transpose(1, 0, 2)


def on_device(
    qkv_rows,
    row_request,
    request_owner,
    cached_len,
    page_table,
    kv_pages,
    residual,
    out_weight,
    norm_gain,
):
    row_count = qkv_rows.shape[0]
    head_cols = qkv_rows.shape[2]
    heads_here = head_cols // HEAD_SIZE
    devices = lax.axis_size("req")
    slot_cap = 5 * row_count // (2 * devices)
    buffer_len = devices * slot_cap
    device_ids = jnp.arange(devices, dtype=jnp.int32)
    matches = row_request[:, None] == device_ids[None, :]
    owner_dev = jnp.sum(jnp.where(matches, request_owner[None, :], 0), axis=1)
    sends_to = (owner_dev[:, None] == device_ids[None, :]).astype(jnp.int32)
    earlier = jnp.cumsum(sends_to, axis=0) - sends_to
    slot_in = jnp.sum(earlier * sends_to, axis=1)
    target = owner_dev * slot_cap + slot_in
    counts = jnp.sum(sends_to, axis=0)
    outgoing = jnp.zeros((buffer_len, 3, head_cols), qkv_rows.dtype).at[target].set(qkv_rows)
    length = cached_len[0]
    pool_pages = kv_pages[page_table[0]]
    cache_span = pool_pages.shape[0] * pool_pages.shape[2]
    cache_keys = pool_pages[:, 0].reshape(cache_span, heads_here, HEAD_SIZE)
    cache_values = pool_pages[:, 1].reshape(cache_span, heads_here, HEAD_SIZE)
    arrived, arrived_counts = (
        lax.all_to_all(
            outgoing.reshape(devices, slot_cap, 3, head_cols),
            "req",
            split_axis=0,
            concat_axis=0,
            tiled=True,
        ),
        lax.all_to_all(counts, "req", split_axis=0, concat_axis=0, tiled=True),
    )
    live_slot = (jnp.arange(slot_cap, dtype=jnp.int32)[None, :] < arrived_counts[:, None]).reshape(
        buffer_len
    )
    live_int = live_slot.astype(jnp.int32)
    new_rank = jnp.cumsum(live_int) - live_int
    cosine, sine_tab = rope_tables(length + new_rank)
    cache_ok = jnp.broadcast_to(
        (jnp.arange(cache_span, dtype=jnp.int32) < length)[None, :], (buffer_len, cache_span)
    )
    new_ok = live_slot[None, :] & (new_rank[None, :] <= new_rank[:, None])
    visible = jnp.concatenate([cache_ok, new_ok], axis=1)
    cosine, sine_tab, visible = (cosine, sine_tab, visible)
    grouped = arrived.reshape(buffer_len, 3, heads_here, HEAD_SIZE)
    result = attend_heads(grouped, cache_keys, cache_values, cosine, sine_tab, visible)
    returned = lax.all_to_all(
        result.reshape(devices, slot_cap, head_cols), "req", split_axis=0, concat_axis=0, tiled=True
    )
    attn_rows = returned.reshape(buffer_len, head_cols)[target]
    partial_sum = jnp.dot(attn_rows, out_weight, preferred_element_type=jnp.float32)
    share_cols = residual.shape[1]
    whole_sum = lax.psum(partial_sum.astype(jnp.bfloat16), "tp").astype(jnp.float32)
    mixed_cols = lax.dynamic_slice_in_dim(
        whole_sum, lax.axis_index("tp") * share_cols, share_cols, 1
    )
    hidden = residual.astype(jnp.float32) + mixed_cols
    square_sum = lax.psum(jnp.sum(hidden * hidden, axis=1), "tp")
    inv_rms = lax.rsqrt(square_sum / D + EPS)
    normed = hidden * inv_rms[:, None] * norm_gain.astype(jnp.float32)[None, :]
    return (hidden.astype(jnp.bfloat16), normed.astype(jnp.bfloat16))


def solution(mesh):
    return jax.shard_map(
        on_device,
        mesh=mesh,
        in_specs=(
            P("req", None, "tp"),
            P("req"),
            P(),
            P("req"),
            P("req", None),
            P("req", None, None, "tp"),
            P("req", "tp"),
            P("tp", None),
            P("tp"),
        ),
        out_specs=(P("req", "tp"), P("req", "tp")),
        check_vma=False,
    )
```

profile of v0, /device:TPU:8, one launch (start us, length us, event | category | flops | bytes accessed | tf_op | source)
XLA Modules:
  0.0 280.5 jit_solution(1655667734073437765)
XLA Ops:
  9.6 17.4 %all-to-all-start.1 = ((s32[128,1,1]{2,1,0:T(1,128)}), s32[128,1,1]{2,1,0:T(1,128)S(1)}, u32[]{:S(2)}, u32[]{:S(2)}) async-start(s32[128,1,1]{2,1,0:T(1,128)} %copy.41), calls=%async_computation.1 | async-start | bytes 131072 | tf_op jit(solution)/shard_map/all_to_all | solution.py:101
  30.3 27.1 %scatter_fusion = bf16[640,3,384]{2,1,0:T(4,128)(2,1)} fusion(bf16[640,3,384]{2,1,0:T(4,128)(2,1)} %broadcast_in_dim.25, s32[256]{0:T(256)S(1)} %bitcast.92, bf16[256,3,384]{2,1,0:T(4,128)(2,1)S(1)} %copy.39), kind=kCustom, calls=%fused_computation.2 | custom fusion | bytes 1770496 | tf_op jit(solution)/shard_map/scatter | solution.py:87
  57.5 14.4 %all-to-all-start = ((bf16[128,5,3,384]{3,2,1,0:T(4,128)(2,1)}), bf16[128,5,3,384]{3,2,1,0:T(4,128)(2,1)}, u32[]{:S(2)}, u32[]{:S(2)}) async-start(bf16[128,5,3,384]{3,2,1,0:T(4,128)(2,1)} %bitcast.86), calls=%async_computation | async-start | bytes 3932160 | tf_op jit(solution)/shard_map/all_to_all | solution.py:94
  72.6 3.3 %gather_fusion = bf16[8,2,128,384]{3,2,1,0:T(8,128)(2,1)} fusion(bf16[8,2,128,384]{3,2,1,0:T(8,128)(2,1)} %param.16, s32[1024]{0:T(1024)S(1)} %pad_clamp_fusion.1), kind=kCustom, calls=%fused_computation | custom fusion | bytes 3145760 | tf_op jit(solution)/shard_map/gather | solution.py:89
  75.9 2.8 fusion.29
  84.4 2.4 reduce
  90.8 30.4 %all-to-all-done = bf16[128,5,3,384]{3,2,1,0:T(4,128)(2,1)} async-done(((bf16[128,5,3,384]{3,2,1,0:T(4,128)(2,1)}), bf16[128,5,3,384]{3,2,1,0:T(4,128)(2,1)}, u32[]{:S(2)}, u32[]{:S(2)}) %all-to-all-start) | async-done | bytes 1474592 | tf_op jit(solution)/shard_map/all_to_all | solution.py:94
  121.3 5.9 %reshape.198 = bf16[640,3,4,96]{3,2,1,0:T(4,128)(2,1)} reshape(bf16[128,5,3,384]{3,2,1,0:T(4,128)(2,1)} %all-to-all-done) | data formatting | bytes 2949120 | tf_op jit(solution)/shard_map/reshape | solution.py:115
  127.2 2.7 slice_bitcast_fusion
  131.5 2.7 fusion.16
  139.4 2.5 maximum_bitcast_fusion
  143.1 22.0 %while.10 = (s32[]{:T(128)}, bf16[4,640,96]{1,2,0:T(8,128)(2,1)}, bf16[4,640,96]{2,1,0:T(8,128)(2,1)}, bf16[4,1664,96]{1,2,0:T(8,128)(2,1)}, pred[640,1664]{1,0:...) while((s32[]{:T(128)}, bf16[4,640,96]{1,2,0:T(8,128)(2,1)}, bf16[4,640,96]{2,1,0:T(8,128)(2,1)}, ...), condition=%wide.region_11.12_spmd, body=%wide.region_8.11_spmd.sunk | while | flops 417524480 | bytes 14785109 | solution.py:51
  143.1 2.1 fusion.37
  145.9 2.6 fusion.39
  148.6 2.1 fusion.37
  151.4 2.7 fusion.39
  154.1 2.1 fusion.37
  156.9 2.6 fusion.39
  159.6 2.1 fusion.37
  162.4 2.6 fusion.39
  168.4 7.9 %all-to-all-start.2 = ((bf16[128,5,384]{2,1,0:T(8,128)(2,1)}), bf16[128,5,384]{2,1,0:T(8,128)(2,1)}, u32[]{:S(2)}, u32[]{:S(2)}) async-start(bf16[128,5,384]{2,1,0:T(8,128)(2,1)} %reshape.200), calls=%async_computation.2 | async-start | bytes 1572864 | tf_op jit(solution)/shard_map/all_to_all | solution.py:117
  176.4 25.5 %all-to-all-done.2 = bf16[128,5,384]{2,1,0:T(8,128)(2,1)} async-done(((bf16[128,5,384]{2,1,0:T(8,128)(2,1)}), bf16[128,5,384]{2,1,0:T(8,128)(2,1)}, u32[]{:S(2)}, u32[]{:S(2)}) %all-to-all-start.2) | async-done | bytes 491552 | tf_op jit(solution)/shard_map/all_to_all | solution.py:117
  207.2 53.7 %all-reduce.2.cloned.1.call-done = bf16[256,3072]{1,0:T(8,128)(2,1)} async-done(((bf16[256,3072]{1,0:T(8,128)(2,1)}), bf16[256,3072]{1,0:T(8,128)(2,1)}) %all-reduce.2.cloned.1.call-update) | async-done | bytes 1572880 | tf_op jit(solution)/shard_map/psum | solution.py:123
  262.1 9.5 %psum.15 = f32[256]{0:T(256)S(1)} all-reduce(f32[256]{0:T(256)S(1)} %multiply_reduce_fusion), channel_id=1, replica_groups=mesh['req'=128,'tp'=4] {'tp'}, use_global_device_ids=true, to_apply=%region_14.15 | all-reduce | flops 256 | bytes 2048 | tf_op jit(solution)/shard_map/psum | solution.py:128
  (77 shorter events, 38.4 us)
Async XLA Ops:
  7.2 197.3 %copy-start = (bf16[384,3072]{1,0:T(8,128)(2,1)S(1)}, bf16[384,3072]{1,0:T(8,128)(2,1)}, u32[]{:S(2)}) copy-start(bf16[384,3072]{1,0:T(8,128)(2,1)} %param.18) | copy-start | bytes 7077892
  9.6 47.9 %all-to-all-start.1 = ((s32[128,1,1]{2,1,0:T(1,128)}), s32[128,1,1]{2,1,0:T(1,128)S(1)}, u32[]{:S(2)}, u32[]{:S(2)}) async-start(s32[128,1,1]{2,1,0:T(1,128)} %copy.41), calls=%async_computation.1 | async-start | bytes 131072 | tf_op jit(solution)/shard_map/all_to_all | solution.py:101
  57.5 15.1 %copy-start.8 = (s32[1,8]{1,0:T(1,128)S(1)}, s32[1,8]{1,0:T(1,128)}, u32[]{:S(2)}) copy-start(s32[1,8]{1,0:T(1,128)} %param.15) | copy-start | bytes 100
  57.5 63.8 %all-to-all-start = ((bf16[128,5,3,384]{3,2,1,0:T(4,128)(2,1)}), bf16[128,5,3,384]{3,2,1,0:T(4,128)(2,1)}, u32[]{:S(2)}, u32[]{:S(2)}) async-start(bf16[128,5,3,384]{3,2,1,0:T(4,128)(2,1)} %bitcast.86), calls=%async_computation | async-start | bytes 3932160 | tf_op jit(solution)/shard_map/all_to_all | solution.py:94
  129.9 1.5 copy-start.1
  129.9 1.6 copy-start.5
  129.9 1.7 copy-start.6
  139.4 2.5 copy-start.2
  139.4 2.5 copy-start.3
  168.4 33.4 %all-to-all-start.2 = ((bf16[128,5,384]{2,1,0:T(8,128)(2,1)}), bf16[128,5,384]{2,1,0:T(8,128)(2,1)}, u32[]{:S(2)}, u32[]{:S(2)}) async-start(bf16[128,5,384]{2,1,0:T(8,128)(2,1)} %reshape.200), calls=%async_computation.2 | async-start | bytes 1572864 | tf_op jit(solution)/shard_map/all_to_all | solution.py:117
  176.3 84.6 %all-reduce.2.cloned.1.call-start = ((), (), s32[]{:S(2)}) async-start(), calls=%async_computation.3 | async-start | bytes 3145728 | tf_op jit(solution)/shard_map/psum | solution.py:123
  206.6 0.7 copy-start.7
  206.6 54.4 %copy-start.4 = (bf16[256,768]{1,0:T(8,128)(2,1)S(1)}, bf16[256,768]{1,0:T(8,128)(2,1)}, u32[]{:S(2)}) copy-start(bf16[256,768]{1,0:T(8,128)(2,1)} %param.17) | copy-start | bytes 1179652
Sparse Core Ops, SparseCore 0:
  206.7 54.1 all-reduce.1
where the time goes:
time: 282 us; the launch traced here: 281 us
  waiting for transfers between devices  110 us (39%)
  local copies, waits for them, and re-layouts  61.6 us (22%)
  starting transfers between devices  39.7 us (14%)
  other arithmetic  24 us (9%)
  matrix products  21.3 us (8%)
  between operations  14.9 us (5%)
  blocking collectives  9.53 us (3%)
    psum x1, waiting for transfers between devices, on_device(): lax.psum(partial_sum.astype(jnp.bfloat16), 'tp').astype(jnp.float32)  53.7 us
    all_to_all x1, waiting for transfers between devices, on_device(): lax.all_to_all(outgoing.reshape(devices, slot_cap, 3, head_cols), 'req',...  30.4 us
    scatter x1, local copies, waits for them, and re-layouts, on_device(): jnp.zeros((buffer_len, 3, head_cols), qkv_rows.dtype).at[target]  27.1 us
    all_to_all x1, waiting for transfers between devices, on_device(): lax.all_to_all(result.reshape(devices, slot_cap, head_cols), 'req', split...  25.5 us
    all_to_all x1, starting transfers between devices, on_device(): lax.all_to_all(counts, 'req', split_axis=0, concat_axis=0, tiled=True)  17.4 us
    all_to_all x1, starting transfers between devices, on_device(): lax.all_to_all(outgoing.reshape(devices, slot_cap, 3, head_cols), 'req',...  14.4 us
    dot_general x4, matrix products, one_head(): jnp.einsum('mk,kd->md', softmax_weights, head_values, preferred_element_t...  10.6 us
    psum x1, blocking collectives, on_device(): square_sum = lax.psum(jnp.sum(hidden * hidden, axis=1), 'tp')  9.53 us
  transfers between devices with their start and end apart: 4, of which 3 were waited for; matrix products, arithmetic and copies ran while one was open for 17% of the time, Pallas kernels for 0%

commit v1 on v0

--- a/solution.py
+++ b/solution.py
@@ -8,6 +8,12 @@
 HEAD_SIZE = 96
 ROPE_BASE = 10000.0
 EPS = 1e-05
+
+
+def add_all(array, axis):
+    pieces = lax.all_gather(array, axis, axis=0, tiled=False)
+    acc = pieces.sum(axis=0)
+    return acc
 
 
 def rope_tables(position):
@@ -120,7 +126,7 @@
     attn_rows = returned.reshape(buffer_len, head_cols)[target]
     partial_sum = jnp.dot(attn_rows, out_weight, preferred_element_type=jnp.float32)
     share_cols = residual.shape[1]
-    whole_sum = lax.psum(partial_sum.astype(jnp.bfloat16), "tp").astype(jnp.float32)
+    whole_sum = add_all(partial_sum.astype(jnp.bfloat16), "tp").astype(jnp.float32)
     mixed_cols = lax.dynamic_slice_in_dim(
         whole_sum, lax.axis_index("tp") * share_cols, share_cols, 1
     )

time: 282 us -> 297 us (1.053)
  waiting for transfers between devices: 110 us -> 119 us
  other arithmetic: 24 us -> 29.5 us
    all_gather x0 -> x1, waiting for transfers between devices: none -> 63.5 us  [add_all(): pieces = lax.all_gather(array, axis, axis=0, tiled=False)]
    psum x1 -> x0, waiting for transfers between devices: 53.7 us -> none  [on_device(): lax.psum(partial_sum.astype(jnp.bfloat16), 'tp').astype(jnp.float32)]
    reduce_sum x0 -> x1, other arithmetic: none -> 5.52 us  [add_all(): acc = pieces.sum(axis=0)]
  transfers between devices with their start and end apart: 4 -> 4, of which waited for: 3 -> 3; matrix products, arithmetic and copies ran while one was open for 17% -> 16% of each run, Pallas kernels for 0% -> 0%
where the time goes in v1:
time: 297 us; the launch traced here: 296 us
  waiting for transfers between devices  119 us (40%)
  local copies, waits for them, and re-layouts  61.6 us (21%)
  starting transfers between devices  39.7 us (13%)
  other arithmetic  29.5 us (10%)
  matrix products  21.3 us (7%)
  between operations  14.9 us (5%)
  blocking collectives  9.19 us (3%)
    all_gather x1, waiting for transfers between devices, add_all(): pieces = lax.all_gather(array, axis, axis=0, tiled=False)  63.5 us
    all_to_all x1, waiting for transfers between devices, on_device(): lax.all_to_all(outgoing.reshape(devices, slot_cap, 3, head_cols), 'req',...  30.4 us
    scatter x1, local copies, waits for them, and re-layouts, on_device(): jnp.zeros((buffer_len, 3, head_cols), qkv_rows.dtype).at[target]  27.1 us
    all_to_all x1, waiting for transfers between devices, on_device(): lax.all_to_all(result.reshape(devices, slot_cap, head_cols), 'req', split...  25.5 us
    all_to_all x1, starting transfers between devices, on_device(): lax.all_to_all(counts, 'req', split_axis=0, concat_axis=0, tiled=True)  17.4 us
    all_to_all x1, starting transfers between devices, on_device(): lax.all_to_all(outgoing.reshape(devices, slot_cap, 3, head_cols), 'req',...  14.4 us
    dot_general x4, matrix products, one_head(): jnp.einsum('mk,kd->md', softmax_weights, head_values, preferred_element_t...  10.6 us
    psum x1, blocking collectives, on_device(): square_sum = lax.psum(jnp.sum(hidden * hidden, axis=1), 'tp')  9.19 us
  transfers between devices with their start and end apart: 4, of which 3 were waited for; matrix products, arithmetic and copies ran while one was open for 16% of the time, Pallas kernels for 0%

profile of v1, /device:TPU:8, one launch (start us, length us, event | category | flops | bytes accessed | tf_op | source)
XLA Modules:
  0.0 295.6 jit_solution(5076373761598278166)
XLA Ops:
  9.6 17.4 %all-to-all-start.1 = ((s32[128,1,1]{2,1,0:T(1,128)}), s32[128,1,1]{2,1,0:T(1,128)S(1)}, u32[]{:S(2)}, u32[]{:S(2)}) async-start(s32[128,1,1]{2,1,0:T(1,128)} %copy.41), calls=%async_computation.1 | async-start | bytes 131072 | tf_op jit(solution)/shard_map/all_to_all | solution.py:107
  30.3 27.1 %scatter_fusion = bf16[640,3,384]{2,1,0:T(4,128)(2,1)} fusion(bf16[640,3,384]{2,1,0:T(4,128)(2,1)} %broadcast_in_dim.25, s32[256]{0:T(256)S(1)} %bitcast.94, bf16[256,3,384]{2,1,0:T(4,128)(2,1)S(1)} %copy.39), kind=kCustom, calls=%fused_computation.2 | custom fusion | bytes 1770496 | tf_op jit(solution)/shard_map/scatter | solution.py:93
  57.5 14.4 %all-to-all-start = ((bf16[128,5,3,384]{3,2,1,0:T(4,128)(2,1)}), bf16[128,5,3,384]{3,2,1,0:T(4,128)(2,1)}, u32[]{:S(2)}, u32[]{:S(2)}) async-start(bf16[128,5,3,384]{3,2,1,0:T(4,128)(2,1)} %bitcast.87), calls=%async_computation | async-start | bytes 3932160 | tf_op jit(solution)/shard_map/all_to_all | solution.py:100
  72.6 3.3 %gather_fusion = bf16[8,2,128,384]{3,2,1,0:T(8,128)(2,1)} fusion(bf16[8,2,128,384]{3,2,1,0:T(8,128)(2,1)} %param.16, s32[1024]{0:T(1024)S(1)} %pad_clamp_fusion.1), kind=kCustom, calls=%fused_computation | custom fusion | bytes 3145760 | tf_op jit(solution)/shard_map/gather | solution.py:95
  75.9 2.8 fusion.29
  84.4 2.4 reduce.1
  90.8 30.4 %all-to-all-done = bf16[128,5,3,384]{3,2,1,0:T(4,128)(2,1)} async-done(((bf16[128,5,3,384]{3,2,1,0:T(4,128)(2,1)}), bf16[128,5,3,384]{3,2,1,0:T(4,128)(2,1)}, u32[]{:S(2)}, u32[]{:S(2)}) %all-to-all-start) | async-done | bytes 1474592 | tf_op jit(solution)/shard_map/all_to_all | solution.py:100
  121.3 5.9 %reshape.198 = bf16[640,3,4,96]{3,2,1,0:T(4,128)(2,1)} reshape(bf16[128,5,3,384]{3,2,1,0:T(4,128)(2,1)} %all-to-all-done) | data formatting | bytes 2949120 | tf_op jit(solution)/shard_map/reshape | solution.py:121
  127.2 2.7 slice_bitcast_fusion
  131.5 2.7 fusion.16
  139.4 2.5 maximum_bitcast_fusion
  143.1 22.0 %while.10 = (s32[]{:T(128)}, bf16[4,640,96]{1,2,0:T(8,128)(2,1)}, bf16[4,640,96]{2,1,0:T(8,128)(2,1)}, bf16[4,1664,96]{1,2,0:T(8,128)(2,1)}, pred[640,1664]{1,0:...) while((s32[]{:T(128)}, bf16[4,640,96]{1,2,0:T(8,128)(2,1)}, bf16[4,640,96]{2,1,0:T(8,128)(2,1)}, ...), condition=%wide.region_11.12_spmd, body=%wide.region_8.11_spmd.sunk | while | flops 417524480 | bytes 14785109 | solution.py:57
  143.1 2.1 fusion.37
  145.9 2.6 fusion.39
  148.6 2.1 fusion.37
  151.4 2.7 fusion.39
  154.1 2.1 fusion.37
  156.9 2.6 fusion.39
  162.4 2.6 fusion.39
  168.4 7.9 %all-to-all-start.2 = ((bf16[128,5,384]{2,1,0:T(8,128)(2,1)}), bf16[128,5,384]{2,1,0:T(8,128)(2,1)}, u32[]{:S(2)}, u32[]{:S(2)}) async-start(bf16[128,5,384]{2,1,0:T(8,128)(2,1)} %reshape.200), calls=%async_computation.2 | async-start | bytes 1572864 | tf_op jit(solution)/shard_map/all_to_all | solution.py:123
  176.4 25.5 %all-to-all-done.2 = bf16[128,5,384]{2,1,0:T(8,128)(2,1)} async-done(((bf16[128,5,384]{2,1,0:T(8,128)(2,1)}), bf16[128,5,384]{2,1,0:T(8,128)(2,1)}, u32[]{:S(2)}, u32[]{:S(2)}) %all-to-all-start.2) | async-done | bytes 491552 | tf_op jit(solution)/shard_map/all_to_all | solution.py:123
  207.2 63.5 %all-gather.3.cloned.1.call-done = bf16[1024,3072]{1,0:T(8,128)(2,1)} async-done(((bf16[256,3072]{1,0:T(8,128)(2,1)}), bf16[1024,3072]{1,0:T(8,128)(2,1)}) %all-gather.3.cloned.1.call-update) | async-done | bytes 6291472 | tf_op jit(solution)/shard_map/all_gather | solution.py:14
  270.8 5.5 %reduce_sum.60 = bf16[256,3072]{1,0:T(8,128)(2,1)} reduce(bf16[4,256,3072]{2,1,0:T(8,128)(2,1)} %bitcast.88, bf16[]{:T(256)} %constant.23.clone.1), dimensions={0}, to_apply=%region_12.13 | reduce | flops 2359296 | bytes 7864322 | tf_op jit(solution)/shard_map/reduce_sum | solution.py:15
  277.5 9.2 %psum.7 = f32[256]{0:T(256)S(1)} all-reduce(f32[256]{0:T(256)S(1)} %multiply_reduce_fusion), channel_id=1, replica_groups=mesh['req'=128,'tp'=4] {'tp'}, use_global_device_ids=true, to_apply=%region_14.15 | all-reduce | flops 256 | bytes 2048 | tf_op jit(solution)/shard_map/psum | solution.py:134
  (78 shorter events, 40.5 us)
Async XLA Ops:
  7.2 197.3 %copy-start = (bf16[384,3072]{1,0:T(8,128)(2,1)S(1)}, bf16[384,3072]{1,0:T(8,128)(2,1)}, u32[]{:S(2)}) copy-start(bf16[384,3072]{1,0:T(8,128)(2,1)} %param.18) | copy-start | bytes 7077892
  9.6 47.9 %all-to-all-start.1 = ((s32[128,1,1]{2,1,0:T(1,128)}), s32[128,1,1]{2,1,0:T(1,128)S(1)}, u32[]{:S(2)}, u32[]{:S(2)}) async-start(s32[128,1,1]{2,1,0:T(1,128)} %copy.41), calls=%async_computation.1 | async-start | bytes 131072 | tf_op jit(solution)/shard_map/all_to_all | solution.py:107
  57.5 15.1 %copy-start.8 = (s32[1,8]{1,0:T(1,128)S(1)}, s32[1,8]{1,0:T(1,128)}, u32[]{:S(2)}) copy-start(s32[1,8]{1,0:T(1,128)} %param.15) | copy-start | bytes 100
  57.5 63.8 %all-to-all-start = ((bf16[128,5,3,384]{3,2,1,0:T(4,128)(2,1)}), bf16[128,5,3,384]{3,2,1,0:T(4,128)(2,1)}, u32[]{:S(2)}, u32[]{:S(2)}) async-start(bf16[128,5,3,384]{3,2,1,0:T(4,128)(2,1)} %bitcast.87), calls=%async_computation | async-start | bytes 3932160 | tf_op jit(solution)/shard_map/all_to_all | solution.py:100
  129.9 1.5 copy-start.1
  129.9 1.6 copy-start.5
  129.9 1.7 copy-start.6
  139.4 2.5 copy-start.2
  139.4 2.5 copy-start.3
  168.4 33.4 %all-to-all-start.2 = ((bf16[128,5,384]{2,1,0:T(8,128)(2,1)}), bf16[128,5,384]{2,1,0:T(8,128)(2,1)}, u32[]{:S(2)}, u32[]{:S(2)}) async-start(bf16[128,5,384]{2,1,0:T(8,128)(2,1)} %reshape.200), calls=%async_computation.2 | async-start | bytes 1572864 | tf_op jit(solution)/shard_map/all_to_all | solution.py:123
  176.3 94.5 %all-gather.3.cloned.1.call-start = ((), (), s32[]{:S(2)}) async-start(), calls=%async_computation.3 | async-start | bytes 7864320 | tf_op jit(solution)/shard_map/all_gather | solution.py:14
  206.6 0.7 copy-start.7
  270.8 5.5 %copy-start.4 = (bf16[256,768]{1,0:T(8,128)(2,1)S(1)}, bf16[256,768]{1,0:T(8,128)(2,1)}, u32[]{:S(2)}) copy-start(bf16[256,768]{1,0:T(8,128)(2,1)} %param.17) | copy-start | bytes 1179652
Sparse Core Ops, SparseCore 0:
  206.7 64.0 all-gather.2
